TPU v7x, 128 devices: a whole 4x4x4 slice. The times are simulated.
128 devices in a mesh: wide: 16 (over x, y_hi, core), narrow: 8 (over z, y_lo).
Axes of the slice: x: 4, y: 4 (y_hi: 2, y_lo: 2; y = y_hi * 2 + y_lo), z: 4, core: 2. Of those that a mesh axis runs over, the one named last changes fastest.
Arguments:
- hidden_in: bfloat16 [128, 8192], P('narrow', 'wide'), may hold values from -75 to 75
- lengths: int32 [128], P('wide'), may hold values from 32 to 8192, as said below
- kv_cache: bfloat16 [2, 2, 152576, 1024], P(None, None, 'wide', 'narrow'), may hold values from -210 to 210, as said below
- qkv_weight: bfloat16 [8192, 8, 1280], P('wide', 'narrow'), may hold values from -0.0625 to 0.0625
- o_weight: bfloat16 [8192, 8192], P('narrow', 'wide'), may hold values from -0.0625 to 0.0625
- gate_up: bfloat16 [8192, 2, 28672], P('wide', None, 'narrow'), may hold values from -0.0625 to 0.0625
- down_weight: bfloat16 [28672, 8192], P('narrow', 'wide'), may hold values from -0.03125 to 0.03125
- attn_gain: bfloat16 [8192], P('wide'), may hold values from 0.099609375 to 1.8984375
- mlp_gain: bfloat16 [8192], P('wide'), may hold values from 0.099609375 to 1.8984375
Outputs:
- hidden_out: bfloat16 [128, 8192], P('narrow', 'wide')
- new_entries: bfloat16 [2, 2, 128, 1024], P(None, None, 'wide', 'narrow')
Inputs may be any that keep to these rules, and one draw needn't show every extreme that they name: Exactly 8 requests have 8192 cached tokens, no two in the same aligned block of 8 requests; every other request has 32 to 192. The lengths of each aligned block of 8 requests sum to at most 9536, and those of one block to exactly 9536. `kv_cache`: cache positions that no request owns hold no live entries.
All inputs are finite; a program needn't handle non-finite values.
Results may differ from a plain program's by a relative error of at most 0.017.
Values may be sent and summed in bfloat16 or wider, within the bound.
No kernel may reach another device: no remote copies, remote signals or barrier semaphores. Data moves between devices by JAX's collectives and lax.ppermute only.
A program may use at most 128 MiB of HBM per device.

v0:
```python
import math
import jax
import jax.numpy as jnp
from jax import lax
from jax.sharding import PartitionSpec as P

D = 8192
HD = 128
LAYERS = 2
EPSILON = 1e-05
ROPE_BASE = 500000.0


def copy_for_each(shard, axis):
    length = lax.axis_size(axis)
    return lax.all_to_all(
        jnp.broadcast_to(shard[None], (length, *shard.shape)), axis, 0, 0, tiled=True
    )


def of_everyone(shard, axis):
    return copy_for_each(shard, axis).sum(axis=0)


def laid_out(parts, dim):
    parts = jnp.moveaxis(parts, 0, dim)
    lengths = parts.shape
    return parts.reshape(*lengths[:dim], lengths[dim] * lengths[dim + 1], *lengths[dim + 2 :])


def gathered_copies(shard, axis, dim):
    parts = copy_for_each(shard, axis)
    return laid_out(parts, dim)


def in_blocks(shard, dim, length):
    before, after = (shard.shape[:dim], shard.shape[dim + 1 :])
    return jnp.moveaxis(shard.reshape(*before, length, -1, *after), dim, 0)


def summed_on_arrival(shard, axis, dim):
    parts = in_blocks(shard, dim, lax.axis_size(axis))
    arrived = lax.all_to_all(parts, axis, split_axis=0, concat_axis=0, tiled=True)
    return arrived.sum(axis=0)


def sent_and_summed(shard, axis, dim):
    length = lax.axis_size(axis)
    parts = lax.all_to_all(in_blocks(shard, dim, length), axis, 0, 0, tiled=True)
    return jnp.sum(parts.astype(jnp.float32), axis=0)


def scale_rows(floats, square_sum, gain):
    scaled = (
        floats * lax.rsqrt(square_sum / D + EPSILON)[:, None] * gain.astype(jnp.float32)[None, :]
    )
    return scaled.astype(jnp.bfloat16)


def norm_rows(stream, gain):
    floats = stream.astype(jnp.float32)
    square_sum = lax.psum(jnp.sum(floats * floats, axis=1), "wide")
    return lax.all_gather(scale_rows(floats, square_sum, gain), "narrow", axis=0, tiled=True)


def rotate_pairs(vectors, cosine, sine_table):
    half_dim = vectors.shape[-1] // 2
    first_half = vectors[..., :half_dim]
    second_half = vectors[..., half_dim:]
    return jnp.concatenate(
        [
            first_half * cosine - second_half * sine_table,
            second_half * cosine + first_half * sine_table,
        ],
        axis=-1,
    )


def rotary_tables(lengths, head_dim):
    half_dim = head_dim // 2
    inverse = jnp.exp(
        jnp.arange(half_dim, dtype=jnp.float32) * (-2.0 * math.log(ROPE_BASE) / head_dim)
    )
    angles = lengths.astype(jnp.float32)[:, None] * inverse[None, :]
    return (jnp.cos(angles), jnp.sin(angles))


def split_heads(projected, lengths, heads_kv, head_dim):
    row_count = projected.shape[0]
    grouped = projected.reshape(row_count, heads_kv, -1, head_dim)
    group_size = grouped.shape[2] - 2
    cosine, sine_table = rotary_tables(lengths, head_dim)
    rotated = rotate_pairs(
        grouped[:, :, : group_size + 1], cosine[:, None, None, :], sine_table[:, None, None, :]
    )
    queries = rotated[:, :, :group_size].astype(jnp.bfloat16)
    key_new = rotated[:, :, group_size].astype(jnp.bfloat16)
    value_new = grouped[:, :, group_size + 1].astype(jnp.bfloat16)
    return (queries, key_new, value_new)


def attend(queries, key_new, value_new, cached_keys, cached_values, lengths):
    row_count, heads_kv, group_size, head_dim = queries.shape
    slot_count = cached_keys.shape[0]
    score_scale = 1.0 / math.sqrt(head_dim)
    key_table = cached_keys.reshape(slot_count, heads_kv, head_dim)
    value_table = cached_values.reshape(slot_count, heads_kv, head_dim)
    starts = jnp.cumsum(lengths) - lengths
    position = jnp.arange(slot_count, dtype=jnp.int32)
    owned = (position[None, :] >= starts[:, None]) & (
        position[None, :] < (starts + lengths)[:, None]
    )
    scores = (
        jnp.einsum("rkgd,tkd->krgt", queries, key_table, preferred_element_type=jnp.float32)
        * score_scale
    )
    scores = jnp.where(owned[None, :, None, :], scores, -jnp.inf)
    own_score = (
        jnp.einsum("rkgd,rkd->krg", queries, key_new, preferred_element_type=jnp.float32)
        * score_scale
    )
    row_peak = jnp.maximum(jnp.max(scores, axis=3), own_score)
    weights = jnp.exp(scores - row_peak[..., None])
    own_weight = jnp.exp(own_score - row_peak)
    weight_sum = jnp.sum(weights, axis=3) + own_weight
    blended = jnp.einsum(
        "krgt,tkd->krgd",
        weights.astype(jnp.bfloat16),
        value_table,
        preferred_element_type=jnp.float32,
    )
    own_rounded = lax.optimization_barrier(own_weight.astype(jnp.bfloat16)).astype(jnp.float32)
    blended = blended + own_rounded[..., None] * jnp.transpose(value_new, (1, 0, 2))[
        :, :, None, :
    ].astype(jnp.float32)
    normalized = (blended / weight_sum[..., None]).astype(jnp.bfloat16)
    return jnp.transpose(normalized, (1, 0, 2, 3)).reshape(
        row_count, heads_kv * group_size * head_dim
    )


def on_device(
    hidden_in, lengths, kv_cache, qkv_weight, o_weight, gate_up, down_weight, attn_gain, mlp_gain
):
    width_dev = hidden_in.shape[1]
    heads_kv = qkv_weight.shape[1]
    flat_qkv = qkv_weight.reshape(width_dev, -1)
    stream = hidden_in
    entries = []
    for layer_index in range(LAYERS):
        normed = norm_rows(stream, attn_gain)
        own_qkv = lax.psum_scatter(
            jnp.dot(normed, flat_qkv, preferred_element_type=jnp.float32),
            "wide",
            scatter_dimension=0,
            tiled=True,
        )
        queries, key_new, value_new = split_heads(own_qkv, lengths, heads_kv, HD)
        own_rows = key_new.shape[0]
        entries.append(
            jnp.stack(
                [
                    key_new.reshape(own_rows, heads_kv * HD),
                    value_new.reshape(own_rows, heads_kv * HD),
                ]
            )
        )
        attended = attend(
            queries, key_new, value_new, kv_cache[layer_index, 0], kv_cache[layer_index, 1], lengths
        )
        heads_all = lax.all_gather(attended, "wide", axis=0, tiled=True)
        summed = lax.psum_scatter(
            jnp.dot(heads_all, o_weight, preferred_element_type=jnp.float32),
            "narrow",
            scatter_dimension=0,
            tiled=True,
        )
        stream = (stream.astype(jnp.float32) + summed).astype(jnp.bfloat16)
        normed = norm_rows(stream, mlp_gain)
        both_parts = jnp.einsum("rd,dkh->rkh", normed, gate_up, preferred_element_type=jnp.float32)
        own_rows_parts = lax.psum_scatter(
            both_parts.astype(jnp.bfloat16), "wide", scatter_dimension=0, tiled=True
        ).astype(jnp.float32)
        activated = (jax.nn.silu(own_rows_parts[:, 0]) * own_rows_parts[:, 1]).astype(jnp.bfloat16)
        partial_down = jnp.dot(
            lax.all_gather(activated, "wide", axis=0, tiled=True),
            down_weight,
            preferred_element_type=jnp.float32,
        )
        summed = lax.psum_scatter(partial_down, "narrow", scatter_dimension=0, tiled=True)
        stream = (stream.astype(jnp.float32) + summed).astype(jnp.bfloat16)
    return (stream, jnp.stack(entries))


def solution(mesh):
    return jax.shard_map(
        on_device,
        mesh=mesh,
        in_specs=(
            P("narrow", "wide"),
            P("wide"),
            P(None, None, "wide", "narrow"),
            P("wide", "narrow", None),
            P("narrow", "wide"),
            P("wide", None, "narrow"),
            P("narrow", "wide"),
            P("wide"),
            P("wide"),
        ),
        out_specs=(P("narrow", "wide"), P(None, None, "wide", "narrow")),
        check_vma=False,
    )
```

profile of v0, /device:TPU:0, one launch (start us, length us, event | category | flops | bytes accessed | tf_op | source)
XLA Modules:
  0.0 797.2 jit_solution(17397242631848850265)
XLA Ops:
  7.2 0.9 fusion.91
  8.2 38.1 %psum.28 = f32[16]{0:T(128)S(1)} all-reduce(f32[16]{0:T(128)S(1)} %fusion.91), channel_id=1, replica_groups=mesh['wide'=16,'narrow'=8] {'wide'}, use_global_device_ids=true, to_apply=%region_2.0 | all-reduce | flops 16 | bytes 128 | tf_op jit(solution)/shard_map/psum | solution.py:62
  46.3 0.7 convert_element_type.205
  46.9 0.8 fusion.93
  47.7 29.7 %all_gather.24 = bf16[128,512]{1,0:T(8,128)(2,1)S(1)} all-gather(bf16[16,512]{1,0:T(8,128)(2,1)S(1)} %fusion.93), channel_id=1, replica_groups=mesh['wide'=16,'narrow'=8] {'narrow'}, dimensions={0}, use_global_device_ids=true | all-gather | bytes 147456 | tf_op jit(solution)/shard_map/all_gather | solution.py:63
  77.4 1.2 fusion.34
  79.1 61.7 %reduce-scatter.13.cloned.1.call-done = f32[8,1280]{1,0:T(8,128)} async-done(((f32[128,1280]{1,0:T(8,128)}), f32[8,1280]{1,0:T(8,128)}) %reduce-scatter.13.cloned.1.call-update) | async-done | bytes 40976 | tf_op jit(solution)/shard_map/reduce_scatter | solution.py:152
  140.9 0.7 fusion.121
  141.5 0.9 fusion.127
  142.8 2.7 fusion.128
  146.1 2.4 fusion.70
  148.6 22.3 %all_gather.25 = bf16[128,1024]{1,0:T(8,128)(2,1)S(1)} all-gather(bf16[8,1024]{1,0:T(8,128)(2,1)S(1)} %bitcast.162), channel_id=1, replica_groups=mesh['wide'=16,'narrow'=8] {'wide'}, dimensions={0}, use_global_device_ids=true | all-gather | bytes 278528 | tf_op jit(solution)/shard_map/all_gather | solution.py:171
  170.9 1.0 fusion.130
  172.0 35.1 %reduce-scatter.15.cloned.1.call-done = f32[16,512]{1,0:T(8,128)} async-done(((f32[128,512]{1,0:T(8,128)}), f32[16,512]{1,0:T(8,128)}) %reduce-scatter.15.cloned.1.call-update) | async-done | bytes 32784 | tf_op jit(solution)/shard_map/reduce_scatter | solution.py:172
  207.1 0.9 fusion.95
  208.0 33.2 %psum.29 = f32[16]{0:T(128)S(1)} all-reduce(f32[16]{0:T(128)S(1)} %get-tuple-element.6), channel_id=1, replica_groups=mesh['wide'=16,'narrow'=8] {'wide'}, use_global_device_ids=true, to_apply=%region_8.9 | all-reduce | flops 16 | bytes 128 | tf_op jit(solution)/shard_map/psum | solution.py:62
  241.2 28.3 %all_gather.26 = bf16[128,512]{1,0:T(8,128)(2,1)S(1)} all-gather(bf16[16,512]{1,0:T(8,128)(2,1)S(1)} %fusion.97), channel_id=1, replica_groups=mesh['wide'=16,'narrow'=8] {'narrow'}, dimensions={0}, use_global_device_ids=true | all-gather | bytes 147456 | tf_op jit(solution)/shard_map/all_gather | solution.py:63
  269.5 4.2 fusion.15
  273.7 1.4 copy.60
  275.3 63.8 %reduce-scatter.25.cloned.1.call-done = bf16[8,7168]{1,0:T(8,128)(2,1)} async-done(((bf16[128,7168]{1,0:T(8,128)(2,1)}), bf16[8,7168]{1,0:T(8,128)(2,1)}) %reduce-scatter.25.cloned.1.call-update) | async-done | bytes 114704
  339.0 0.9 convert_element_type.222
  340.0 24.2 %all_gather.27 = bf16[128,3584]{1,0:T(8,128)(2,1)S(1)} all-gather(bf16[8,3584]{1,0:T(8,128)(2,1)S(1)} %fusion.86), channel_id=1, replica_groups=mesh['wide'=16,'narrow'=8] {'wide'}, dimensions={0}, use_global_device_ids=true | all-gather | bytes 974848 | tf_op jit(solution)/shard_map/all_gather | solution.py:186
  364.2 3.4 fusion.131
  367.6 35.6 %reduce-scatter.17.cloned.1.call-done = f32[16,512]{1,0:T(8,128)} async-done(((f32[128,512]{1,0:T(8,128)}), f32[16,512]{1,0:T(8,128)}) %reduce-scatter.17.cloned.1.call-update) | async-done | bytes 32784 | tf_op jit(solution)/shard_map/reduce_scatter | solution.py:190
  403.2 0.9 fusion.99
  404.1 33.2 %psum.30 = f32[16]{0:T(128)S(1)} all-reduce(f32[16]{0:T(128)S(1)} %get-tuple-element.4), channel_id=1, replica_groups=mesh['wide'=16,'narrow'=8] {'wide'}, use_global_device_ids=true, to_apply=%region_12.13 | all-reduce | flops 16 | bytes 128 | tf_op jit(solution)/shard_map/psum | solution.py:62
  437.4 28.3 %all_gather.28 = bf16[128,512]{1,0:T(8,128)(2,1)S(1)} all-gather(bf16[16,512]{1,0:T(8,128)(2,1)S(1)} %fusion.101), channel_id=1, replica_groups=mesh['wide'=16,'narrow'=8] {'narrow'}, dimensions={0}, use_global_device_ids=true | all-gather | bytes 147456 | tf_op jit(solution)/shard_map/all_gather | solution.py:63
  465.7 1.2 fusion.32
  467.0 59.8 %reduce-scatter.19.cloned.1.call-done = f32[8,1280]{1,0:T(8,128)} async-done(((f32[128,1280]{1,0:T(8,128)}), f32[8,1280]{1,0:T(8,128)}) %reduce-scatter.19.cloned.1.call-update) | async-done | bytes 40976 | tf_op jit(solution)/shard_map/reduce_scatter | solution.py:152
  526.7 0.7 fusion.122
  527.4 0.9 fusion.126
  528.5 2.7 fusion.129
  532.0 2.3 fusion.75
  534.3 22.3 %all_gather.29 = bf16[128,1024]{1,0:T(8,128)(2,1)S(1)} all-gather(bf16[8,1024]{1,0:T(8,128)(2,1)S(1)} %bitcast.163), channel_id=1, replica_groups=mesh['wide'=16,'narrow'=8] {'wide'}, dimensions={0}, use_global_device_ids=true | all-gather | bytes 278528 | tf_op jit(solution)/shard_map/all_gather | solution.py:171
  556.6 1.0 fusion.132
  557.7 35.2 %reduce-scatter.21.cloned.1.call-done = f32[16,512]{1,0:T(8,128)} async-done(((f32[128,512]{1,0:T(8,128)}), f32[16,512]{1,0:T(8,128)}) %reduce-scatter.21.cloned.1.call-update) | async-done | bytes 32784 | tf_op jit(solution)/shard_map/reduce_scatter | solution.py:172
  592.9 0.9 fusion.103
  593.8 33.2 %psum.31 = f32[16]{0:T(128)S(1)} all-reduce(f32[16]{0:T(128)S(1)} %get-tuple-element.2), channel_id=1, replica_groups=mesh['wide'=16,'narrow'=8] {'wide'}, use_global_device_ids=true, to_apply=%region_18.19 | all-reduce | flops 16 | bytes 128 | tf_op jit(solution)/shard_map/psum | solution.py:62
  627.0 28.3 %all_gather.30 = bf16[128,512]{1,0:T(8,128)(2,1)S(1)} all-gather(bf16[16,512]{1,0:T(8,128)(2,1)S(1)} %fusion.105), channel_id=1, replica_groups=mesh['wide'=16,'narrow'=8] {'narrow'}, dimensions={0}, use_global_device_ids=true | all-gather | bytes 147456 | tf_op jit(solution)/shard_map/all_gather | solution.py:63
  655.3 4.2 fusion.12
  659.5 1.4 copy.61
  661.0 63.8 %reduce-scatter.27.cloned.1.call-done = bf16[8,7168]{1,0:T(8,128)(2,1)} async-done(((bf16[128,7168]{1,0:T(8,128)(2,1)}), bf16[8,7168]{1,0:T(8,128)(2,1)}) %reduce-scatter.27.cloned.1.call-update) | async-done | bytes 114704
  724.8 0.9 convert_element_type.240
  725.8 24.2 %all_gather.31 = bf16[128,3584]{1,0:T(8,128)(2,1)S(1)} all-gather(bf16[8,3584]{1,0:T(8,128)(2,1)S(1)} %fusion.84), channel_id=1, replica_groups=mesh['wide'=16,'narrow'=8] {'wide'}, dimensions={0}, use_global_device_ids=true | all-gather | bytes 974848 | tf_op jit(solution)/shard_map/all_gather | solution.py:186
  750.0 3.4 fusion.133
  753.4 0.6 pad_maximum_fusion
  754.0 35.0 %reduce-scatter.23.cloned.1.call-done = f32[16,512]{1,0:T(8,128)} async-done(((f32[128,512]{1,0:T(8,128)}), f32[16,512]{1,0:T(8,128)}) %reduce-scatter.23.cloned.1.call-update) | async-done | bytes 32784 | tf_op jit(solution)/shard_map/reduce_scatter | solution.py:190
  789.0 1.4 fusion.106
  (63 shorter events, 3.1 us)
Async XLA Ops:
  7.2 70.2 %copy-start = (bf16[512,1,1280]{2,0,1:T(8,128)(2,1)S(1)}, bf16[512,1,1280]{2,0,1:T(8,128)(2,1)}, u32[]{:S(2)}) copy-start(bf16[512,1,1280]{2,0,1:T(8,128)(2,1)} %param.12) | copy-start | bytes 3932164
  7.2 71.5 %copy-start.4 = (s32[8]{0:T(128)S(1)}, s32[8]{0:T(128)}, u32[]{:S(2)}) copy-start(s32[8]{0:T(128)} %param.10) | copy-start | bytes 100
  7.2 133.7 %reduce-scatter.13.cloned.1.call-start = ((), (), s32[]{:S(2)}) async-start(), calls=%async_computation.8 | async-start | bytes 696320 | tf_op jit(solution)/shard_map/reduce_scatter | solution.py:152
  78.6 128.5 %reduce-scatter.15.cloned.1.call-start = ((), (), s32[]{:S(2)}) async-start(), calls=%async_computation.9 | async-start | bytes 294912 | tf_op jit(solution)/shard_map/reduce_scatter | solution.py:172
  146.1 24.8 %copy-start.1 = (bf16[1024,512]{1,0:T(8,128)(2,1)S(1)}, bf16[1024,512]{1,0:T(8,128)(2,1)}, u32[]{:S(2)}) copy-start(bf16[1024,512]{1,0:T(8,128)(2,1)} %param.13) | copy-start | bytes 3145732
  146.1 25.8 %copy-start.3 = (bf16[512]{0:T(512)(128)(2,1)S(1)}, bf16[512]{0:T(512)(128)(2,1)}, u32[]{:S(2)}) copy-start(bf16[512]{0:T(512)(128)(2,1)} %param.17) | copy-start | bytes 3076
  146.1 61.0 %copy-start.2 = (bf16[16,512]{1,0:T(8,128)(2,1)S(1)}, bf16[16,512]{1,0:T(8,128)(2,1)}, u32[]{:S(2)}) copy-start(bf16[16,512]{1,0:T(8,128)(2,1)} %param.9) | copy-start | bytes 49156
  171.9 167.1 %reduce-scatter.25.cloned.1.call-start = ((), (), s32[]{:S(2)}) async-start(), calls=%async_computation.14 | async-start | bytes 1949696
  275.2 128.0 %reduce-scatter.17.cloned.1.call-start = ((), (), s32[]{:S(2)}) async-start(), calls=%async_computation.10 | async-start | bytes 294912 | tf_op jit(solution)/shard_map/reduce_scatter | solution.py:190
  367.6 159.2 %reduce-scatter.19.cloned.1.call-start = ((), (), s32[]{:S(2)}) async-start(), calls=%async_computation.11 | async-start | bytes 696320 | tf_op jit(solution)/shard_map/reduce_scatter | solution.py:152
  466.9 126.0 %reduce-scatter.21.cloned.1.call-start = ((), (), s32[]{:S(2)}) async-start(), calls=%async_computation.12 | async-start | bytes 294912 | tf_op jit(solution)/shard_map/reduce_scatter | solution.py:172
  557.7 167.1 %reduce-scatter.27.cloned.1.call-start = ((), (), s32[]{:S(2)}) async-start(), calls=%async_computation.15 | async-start | bytes 1949696
  661.0 128.0 %reduce-scatter.23.cloned.1.call-start = ((), (), s32[]{:S(2)}) async-start(), calls=%async_computation.13 | async-start | bytes 294912 | tf_op jit(solution)/shard_map/reduce_scatter | solution.py:190
Sparse Core Ops, SparseCore 0:
  78.7 62.0 reduce-scatter.12
  172.0 35.0 reduce-scatter.14
  275.3 63.6 reduce-scatter.24
  367.7 35.4 reduce-scatter.16
  467.0 59.6 reduce-scatter.18
  557.8 35.0 reduce-scatter.20
  661.1 63.6 reduce-scatter.26
  753.5 35.4 reduce-scatter.22
where the time goes:
time: 798 us; the launch traced here: 797 us
  waiting for transfers between devices  390 us (49%)
  blocking collectives  345 us (43%)
  matrix products  30.1 us (4%)
  between operations  14.3 us (2%)
  other arithmetic  12.5 us (2%)
    psum x4, blocking collectives, norm_rows(): square_sum = lax.psum(jnp.sum(floats * floats, axis=1), 'wide')  138 us
    unnamed x10, waiting for transfers between devices  128 us
    reduce_scatter x2, waiting for transfers between devices, on_device(): lax.psum_scatter(jnp.dot(normed, flat_qkv, preferred_element_type=jnp.flo...  122 us
    all_gather x4, blocking collectives, norm_rows(): lax.all_gather(scale_rows(floats, square_sum, gain), 'narrow', axis=0, ti...  115 us
    reduce_scatter x2, waiting for transfers between devices, on_device(): lax.psum_scatter(partial_down, 'narrow', scatter_dimension=0, tiled=True)  70.6 us
    reduce_scatter x2, waiting for transfers between devices, on_device(): lax.psum_scatter(jnp.dot(heads_all, o_weight, preferred_element_type=jnp....  70.3 us
    all_gather x2, blocking collectives, on_device(): lax.all_gather(activated, 'wide', axis=0, tiled=True)  48.3 us
    all_gather x2, blocking collectives, on_device(): heads_all = lax.all_gather(attended, 'wide', axis=0, tiled=True)  44.6 us
  transfers between devices with their start and end apart: 8, of which 8 were waited for; matrix products, arithmetic and copies ran while one was open for 0% of the time, Pallas kernels for 0%

commit v1 on v0

--- a/solution.py
+++ b/solution.py
@@ -60,7 +60,15 @@
 def norm_rows(stream, gain):
     floats = stream.astype(jnp.float32)
     square_sum = lax.psum(jnp.sum(floats * floats, axis=1), "wide")
-    return lax.all_gather(scale_rows(floats, square_sum, gain), "narrow", axis=0, tiled=True)
+    return jnp.concatenate(
+        lax.all_to_all(
+            jnp.stack([scale_rows(floats, square_sum, gain)] * lax.axis_size("narrow")),
+            "narrow",
+            0,
+            0,
+        ),
+        axis=0,
+    )
 
 
 def rotate_pairs(vectors, cosine, sine_table):

time: 798 us -> 725 us (0.909)
  blocking collectives: 345 us -> 258 us
    all_gather x4 -> x0, blocking collectives: 115 us -> none  [norm_rows(): lax.all_gather(scale_rows(floats, square_sum, gain), 'narrow', axis=0, ti...]
    all_to_all x0 -> x3, blocking collectives: none -> 27.3 us  [norm_rows(): lax.all_to_all(jnp.stack([scale_rows(floats, square_sum, gain)] * lax.axi...]
  transfers between devices with their start and end apart: 8 -> 9, of which waited for: 8 -> 9; matrix products, arithmetic and copies ran while one was open for 0% -> 0% of each run, Pallas kernels for 0% -> 0%
where the time goes in v1:
time: 725 us; the launch traced here: 724 us
  waiting for transfers between devices  396 us (55%)
  blocking collectives  258 us (36%)
  matrix products  30.1 us (4%)
  between operations  14.3 us (2%)
  other arithmetic  13.9 us (2%)
    psum x4, blocking collectives, norm_rows(): square_sum = lax.psum(jnp.sum(floats * floats, axis=1), 'wide')  138 us
    unnamed x10, waiting for transfers between devices  129 us
    reduce_scatter x2, waiting for transfers between devices, on_device(): lax.psum_scatter(jnp.dot(normed, flat_qkv, preferred_element_type=jnp.flo...  121 us
    reduce_scatter x2, waiting for transfers between devices, on_device(): lax.psum_scatter(partial_down, 'narrow', scatter_dimension=0, tiled=True)  70.6 us
    reduce_scatter x2, waiting for transfers between devices, on_device(): lax.psum_scatter(jnp.dot(heads_all, o_weight, preferred_element_type=jnp....  70.4 us
    all_gather x2, blocking collectives, on_device(): lax.all_gather(activated, 'wide', axis=0, tiled=True)  48.3 us
    all_gather x2, blocking collectives, on_device(): heads_all = lax.all_gather(attended, 'wide', axis=0, tiled=True)  44.6 us
    all_to_all x3, blocking collectives, norm_rows(): lax.all_to_all(jnp.stack([scale_rows(floats, square_sum, gain)] * lax.axi...  27.3 us
  transfers between devices with their start and end apart: 9, of which 9 were waited for; matrix products, arithmetic and copies ran while one was open for 0% of the time, Pallas kernels for 0%

profile of v1, /device:TPU:0, one launch (start us, length us, event | category | flops | bytes accessed | tf_op | source)
XLA Modules:
  0.0 723.5 jit_solution(3692754149465778626)
XLA Ops:
  7.2 0.9 fusion.89
  8.1 38.1 %psum.28 = f32[16]{0:T(128)S(1)} all-reduce(f32[16]{0:T(128)S(1)} %fusion.89), channel_id=1, replica_groups=mesh['wide'=16,'narrow'=8] {'wide'}, use_global_device_ids=true, to_apply=%region_2.0 | all-reduce | flops 16 | bytes 128 | tf_op jit(solution)/shard_map/psum | solution.py:62
  46.2 0.7 convert_element_type.205
  46.9 0.8 fusion.91
  48.3 5.4 all-to-all-start
  53.8 0.8 reduce-window.8
  54.6 0.7 bitcast_subtract_fusion
  55.4 5.1 all-to-all-done
  60.5 1.2 fusion.34
  62.0 60.3 %reduce-scatter.13.cloned.1.call-done = f32[8,1280]{1,0:T(8,128)} async-done(((f32[128,1280]{1,0:T(8,128)}), f32[8,1280]{1,0:T(8,128)}) %reduce-scatter.13.cloned.1.call-update) | async-done | bytes 40976 | tf_op jit(solution)/shard_map/reduce_scatter | solution.py:160
  123.0 0.9 fusion.125
  124.2 2.7 fusion.126
  127.6 2.4 fusion.70
  130.0 22.3 %all_gather.12 = bf16[128,1024]{1,0:T(8,128)(2,1)S(1)} all-gather(bf16[8,1024]{1,0:T(8,128)(2,1)S(1)} %bitcast.170), channel_id=1, replica_groups=mesh['wide'=16,'narrow'=8] {'wide'}, dimensions={0}, use_global_device_ids=true | all-gather | bytes 278528 | tf_op jit(solution)/shard_map/all_gather | solution.py:179
  152.3 1.0 fusion.128
  153.4 35.2 %reduce-scatter.15.cloned.1.call-done = f32[16,512]{1,0:T(8,128)} async-done(((f32[128,512]{1,0:T(8,128)}), f32[16,512]{1,0:T(8,128)}) %reduce-scatter.15.cloned.1.call-update) | async-done | bytes 32784 | tf_op jit(solution)/shard_map/reduce_scatter | solution.py:180
  188.6 0.9 fusion.93
  189.5 33.2 %psum.29 = f32[16]{0:T(128)S(1)} all-reduce(f32[16]{0:T(128)S(1)} %get-tuple-element.6), channel_id=1, replica_groups=mesh['wide'=16,'narrow'=8] {'wide'}, use_global_device_ids=true, to_apply=%region_8.9 | all-reduce | flops 16 | bytes 128 | tf_op jit(solution)/shard_map/psum | solution.py:62
  222.8 9.1 %all_to_all.20 = bf16[8,16,512]{2,1,0:T(8,128)(2,1)S(1)} all-to-all(bf16[8,16,512]{2,1,0:T(8,128)(2,1)S(1)} %stack.19), channel_id=1, replica_groups=mesh['wide'=16,'narrow'=8] {'narrow'}, dimensions={0} | all-to-all | bytes 262144 | tf_op jit(solution)/shard_map/all_to_all | solution.py:64
  231.9 4.2 fusion.15
  236.1 1.4 copy.60
  237.6 64.5 %reduce-scatter.25.cloned.1.call-done = bf16[8,7168]{1,0:T(8,128)(2,1)} async-done(((bf16[128,7168]{1,0:T(8,128)(2,1)}), bf16[8,7168]{1,0:T(8,128)(2,1)}) %reduce-scatter.25.cloned.1.call-update) | async-done | bytes 114704
  302.1 0.9 convert_element_type.222
  303.1 24.2 %all_gather.13 = bf16[128,3584]{1,0:T(8,128)(2,1)S(1)} all-gather(bf16[8,3584]{1,0:T(8,128)(2,1)S(1)} %fusion.84), channel_id=1, replica_groups=mesh['wide'=16,'narrow'=8] {'wide'}, dimensions={0}, use_global_device_ids=true | all-gather | bytes 974848 | tf_op jit(solution)/shard_map/all_gather | solution.py:194
  327.3 3.4 fusion.129
  330.7 35.6 %reduce-scatter.17.cloned.1.call-done = f32[16,512]{1,0:T(8,128)} async-done(((f32[128,512]{1,0:T(8,128)}), f32[16,512]{1,0:T(8,128)}) %reduce-scatter.17.cloned.1.call-update) | async-done | bytes 32784 | tf_op jit(solution)/shard_map/reduce_scatter | solution.py:198
  366.4 0.9 fusion.97
  367.2 33.2 %psum.30 = f32[16]{0:T(128)S(1)} all-reduce(f32[16]{0:T(128)S(1)} %get-tuple-element.4), channel_id=1, replica_groups=mesh['wide'=16,'narrow'=8] {'wide'}, use_global_device_ids=true, to_apply=%region_12.13 | all-reduce | flops 16 | bytes 128 | tf_op jit(solution)/shard_map/psum | solution.py:62
  400.5 9.1 %all_to_all.21 = bf16[8,16,512]{2,1,0:T(8,128)(2,1)S(1)} all-to-all(bf16[8,16,512]{2,1,0:T(8,128)(2,1)S(1)} %stack.20), channel_id=1, replica_groups=mesh['wide'=16,'narrow'=8] {'narrow'}, dimensions={0} | all-to-all | bytes 262144 | tf_op jit(solution)/shard_map/all_to_all | solution.py:64
  409.6 1.2 fusion.32
  410.9 60.6 %reduce-scatter.19.cloned.1.call-done = f32[8,1280]{1,0:T(8,128)} async-done(((f32[128,1280]{1,0:T(8,128)}), f32[8,1280]{1,0:T(8,128)}) %reduce-scatter.19.cloned.1.call-update) | async-done | bytes 40976 | tf_op jit(solution)/shard_map/reduce_scatter | solution.py:160
  472.1 0.9 fusion.124
  473.3 2.7 fusion.127
  476.7 2.3 fusion.75
  479.1 22.3 %all_gather.14 = bf16[128,1024]{1,0:T(8,128)(2,1)S(1)} all-gather(bf16[8,1024]{1,0:T(8,128)(2,1)S(1)} %bitcast.171), channel_id=1, replica_groups=mesh['wide'=16,'narrow'=8] {'wide'}, dimensions={0}, use_global_device_ids=true | all-gather | bytes 278528 | tf_op jit(solution)/shard_map/all_gather | solution.py:179
  501.3 1.0 fusion.130
  502.4 35.2 %reduce-scatter.21.cloned.1.call-done = f32[16,512]{1,0:T(8,128)} async-done(((f32[128,512]{1,0:T(8,128)}), f32[16,512]{1,0:T(8,128)}) %reduce-scatter.21.cloned.1.call-update) | async-done | bytes 32784 | tf_op jit(solution)/shard_map/reduce_scatter | solution.py:180
  537.6 0.9 fusion.101
  538.5 33.2 %psum.31 = f32[16]{0:T(128)S(1)} all-reduce(f32[16]{0:T(128)S(1)} %get-tuple-element.2), channel_id=1, replica_groups=mesh['wide'=16,'narrow'=8] {'wide'}, use_global_device_ids=true, to_apply=%region_18.19 | all-reduce | flops 16 | bytes 128 | tf_op jit(solution)/shard_map/psum | solution.py:62
  571.8 9.1 %all_to_all.22 = bf16[8,16,512]{2,1,0:T(8,128)(2,1)S(1)} all-to-all(bf16[8,16,512]{2,1,0:T(8,128)(2,1)S(1)} %stack.21), channel_id=1, replica_groups=mesh['wide'=16,'narrow'=8] {'narrow'}, dimensions={0} | all-to-all | bytes 262144 | tf_op jit(solution)/shard_map/all_to_all | solution.py:64
  580.9 4.2 fusion.12
  585.1 1.4 copy.61
  586.7 64.5 %reduce-scatter.27.cloned.1.call-done = bf16[8,7168]{1,0:T(8,128)(2,1)} async-done(((bf16[128,7168]{1,0:T(8,128)(2,1)}), bf16[8,7168]{1,0:T(8,128)(2,1)}) %reduce-scatter.27.cloned.1.call-update) | async-done | bytes 114704
  651.2 0.9 convert_element_type.240
  652.2 24.2 %all_gather.15 = bf16[128,3584]{1,0:T(8,128)(2,1)S(1)} all-gather(bf16[8,3584]{1,0:T(8,128)(2,1)S(1)} %fusion.82), channel_id=1, replica_groups=mesh['wide'=16,'narrow'=8] {'wide'}, dimensions={0}, use_global_device_ids=true | all-gather | bytes 974848 | tf_op jit(solution)/shard_map/all_gather | solution.py:194
  676.3 3.4 fusion.131
  680.4 35.0 %reduce-scatter.23.cloned.1.call-done = f32[16,512]{1,0:T(8,128)} async-done(((f32[128,512]{1,0:T(8,128)}), f32[16,512]{1,0:T(8,128)}) %reduce-scatter.23.cloned.1.call-update) | async-done | bytes 32784 | tf_op jit(solution)/shard_map/reduce_scatter | solution.py:198
  715.3 1.4 fusion.104
  (66 shorter events, 5.5 us)
Async XLA Ops:
  7.2 53.3 %copy-start = (bf16[512,1,1280]{2,0,1:T(8,128)(2,1)S(1)}, bf16[512,1,1280]{2,0,1:T(8,128)(2,1)}, u32[]{:S(2)}) copy-start(bf16[512,1,1280]{2,0,1:T(8,128)(2,1)} %param.12) | copy-start | bytes 3932164
  48.3 12.1 %all-to-all-start = ((bf16[8,16,512]{2,1,0:T(8,128)(2,1)}), bf16[8,16,512]{2,1,0:T(8,128)(2,1)S(1)}, u32[]{:S(2)}, u32[]{:S(2)}) async-start(bf16[8,16,512]{2,1,0:T(8,128)(2,1)} %stack.18), calls=%async_computation | async-start | bytes 262144 | tf_op jit(solution)/shard_map/all_to_all | solution.py:64
  53.8 68.5 %reduce-scatter.13.cloned.1.call-start = ((), (), s32[]{:S(2)}) async-start(), calls=%async_computation.12 | async-start | bytes 696320 | tf_op jit(solution)/shard_map/reduce_scatter | solution.py:160
  61.7 127.0 %reduce-scatter.15.cloned.1.call-start = ((), (), s32[]{:S(2)}) async-start(), calls=%async_computation.13 | async-start | bytes 294912 | tf_op jit(solution)/shard_map/reduce_scatter | solution.py:180
  127.5 24.8 %copy-start.1 = (bf16[1024,512]{1,0:T(8,128)(2,1)S(1)}, bf16[1024,512]{1,0:T(8,128)(2,1)}, u32[]{:S(2)}) copy-start(bf16[1024,512]{1,0:T(8,128)(2,1)} %param.13) | copy-start | bytes 3145732
  127.6 25.8 %copy-start.3 = (bf16[512]{0:T(512)(128)(2,1)S(1)}, bf16[512]{0:T(512)(128)(2,1)}, u32[]{:S(2)}) copy-start(bf16[512]{0:T(512)(128)(2,1)} %param.17) | copy-start | bytes 3076
  127.6 61.1 %copy-start.2 = (bf16[16,512]{1,0:T(8,128)(2,1)S(1)}, bf16[16,512]{1,0:T(8,128)(2,1)}, u32[]{:S(2)}) copy-start(bf16[16,512]{1,0:T(8,128)(2,1)} %param.9) | copy-start | bytes 49156
  153.3 148.8 %reduce-scatter.25.cloned.1.call-start = ((), (), s32[]{:S(2)}) async-start(), calls=%async_computation.18 | async-start | bytes 1949696
  237.6 128.8 %reduce-scatter.17.cloned.1.call-start = ((), (), s32[]{:S(2)}) async-start(), calls=%async_computation.14 | async-start | bytes 294912 | tf_op jit(solution)/shard_map/reduce_scatter | solution.py:198
  330.7 140.8 %reduce-scatter.19.cloned.1.call-start = ((), (), s32[]{:S(2)}) async-start(), calls=%async_computation.15 | async-start | bytes 696320 | tf_op jit(solution)/shard_map/reduce_scatter | solution.py:160
  410.8 126.8 %reduce-scatter.21.cloned.1.call-start = ((), (), s32[]{:S(2)}) async-start(), calls=%async_computation.16 | async-start | bytes 294912 | tf_op jit(solution)/shard_map/reduce_scatter | solution.py:180
  502.4 148.8 %reduce-scatter.27.cloned.1.call-start = ((), (), s32[]{:S(2)}) async-start(), calls=%async_computation.19 | async-start | bytes 1949696
  586.6 128.7 %reduce-scatter.23.cloned.1.call-start = ((), (), s32[]{:S(2)}) async-start(), calls=%async_computation.17 | async-start | bytes 294912 | tf_op jit(solution)/shard_map/reduce_scatter | solution.py:198
Sparse Core Ops, SparseCore 0:
  61.8 60.4 reduce-scatter.12
  153.5 35.1 reduce-scatter.14
  237.7 64.3 reduce-scatter.24
  330.8 35.5 reduce-scatter.16
  410.9 60.4 reduce-scatter.18
  502.5 35.1 reduce-scatter.20
  586.7 64.4 reduce-scatter.26
  679.8 35.4 reduce-scatter.22
